TPU v7x, 256 devices: a whole 4x4x8 slice. The times are simulated.
256 devices in a mesh: row: 32 (over y, x, z_hi), col: 8 (over z_lo, core).
Axes of the slice: x: 4, y: 4, z: 8 (z_hi: 2, z_lo: 4; z = z_hi * 4 + z_lo), core: 2. Of those that a mesh axis runs over, the one named last changes fastest.
Arguments:
- rhs: float32 [32, 8, 12, 192, 128], P('row', 'col'), may hold values from -6 to 6
- smoother: bfloat16 [32, 8, 3, 3, 768], P('row', 'col'), may hold values from -0.375 to 2.375
- blocks: bfloat16 [32, 8, 12, 192, 1536], P('row', 'col'), may hold values from -0.15625 to 0.15625
- col_index: int32 [32, 8, 12, 8], P('row', 'col'), may hold values from 0 to 27, as said below
- send_list: int32 [32, 8, 4, 4], P('row', 'col'), may hold values from 0 to 11, as said below
- agg_id: int32 [32, 8, 12], P('row', 'col'), may hold values from 0 to 3, as said below
- prolong: bfloat16 [32, 8, 6, 2304], P('row', 'col'), may hold values from -0.4375 to 0.4375
- coarse_inverse: bfloat16 [6144, 6144], P('row'), may hold values from -0.078125 to 0.078125
Outputs:
- smoothed_solution: float32 [32, 8, 12, 192, 128], P('row', 'col')
Inputs may be any that keep to these rules, and one draw needn't show every extreme that they name: `col_index`: A value below 12 names a block row of the same device; the value 12 + 4 * g + j names slot j of ghost group g. Every ghost slot is named by some entry of each device. `send_list`: the 4 blocks of one device and group are distinct. `agg_id`: every aggregate of a device holds at least one block row.
All inputs are finite; a program needn't handle non-finite values.
Results may differ from a plain program's by a relative error of at most 0.0029.
Values may be sent and summed in bfloat16 or wider, within the bound.
No kernel may reach another device: no remote copies, remote signals or barrier semaphores. Data moves between devices by JAX's collectives and lax.ppermute only.
A program may use at most 64 MiB of HBM per device.

v0:
```python
import jax
import jax.numpy as jnp
from jax import lax
from jax.sharding import PartitionSpec as P

damping = 0.6


def passed_along(value, axis, steps):
    count = lax.axis_size(axis)
    pairs = [(source, (source + steps) % count) for source in range(count)]
    return lax.ppermute(value, axis, pairs)


def point_smooth(coefficients, vector):
    leading = vector.shape[:2]
    blocks = vector.shape[2]
    grains = vector.shape[3] // 3
    columns = vector.shape[4]
    factors = coefficients.astype(jnp.float32).reshape(leading + (3, 3, blocks, grains))
    pieces = vector.reshape(leading + (blocks, 3, grains, columns))
    outputs = []
    for component in range(3):
        summed = factors[:, :, component, 0, :, :, None] * pieces[:, :, :, 0]
        summed = summed + factors[:, :, component, 1, :, :, None] * pieces[:, :, :, 1]
        summed = summed + factors[:, :, component, 2, :, :, None] * pieces[:, :, :, 2]
        outputs.append(summed)
    return damping * jnp.stack(outputs, axis=3).reshape(vector.shape)


def body(rhs, smoother, blocks, col_index, send_list, agg_id, prolong, coarse_inverse):
    block_count = rhs.shape[2]
    dof_count = rhs.shape[3]
    vectors = rhs.shape[4]
    send_rows = send_list[0, 0]
    coarse_dofs = prolong.shape[2]
    shaped = prolong[0, 0].reshape((coarse_dofs, block_count, dof_count))

    def apply_operator(vector, ready_ghosts=None):
        vector_low = vector.astype(jnp.bfloat16)
        shard_low = vector_low[0, 0]
        ghosts = []
        for offset in (1, -1):
            packed = jnp.take(shard_low, send_rows[0 if offset == 1 else 1], axis=0)
            ghosts.append(passed_along(packed, "row", offset))
        for offset in (1, -1):
            packed = jnp.take(shard_low, send_rows[2 if offset == 1 else 3], axis=0)
            ghosts.append(passed_along(packed, "col", offset))
        source = jnp.concatenate([shard_low] + list(ghosts), axis=0)
        columns = col_index[0, 0]
        picked = jnp.take(source, columns.reshape(-1), axis=0).reshape((block_count, -1, vectors))
        product = jnp.einsum(
            "nde,ner->ndr", blocks[0, 0], picked, preferred_element_type=jnp.float32
        )
        return product[None, None]

    first_iter = point_smooth(smoother, rhs)
    residual_first = rhs - apply_operator(first_iter)
    update_second = point_smooth(smoother, residual_first)
    second_iter = first_iter + update_second
    residual_second = residual_first - apply_operator(update_second)
    coarse_rows = coarse_inverse.shape[1] // (lax.axis_size("row") * lax.axis_size("col"))
    aggregates = coarse_rows // coarse_dofs
    onehot = (agg_id[0, 0][None, :] == jnp.arange(aggregates, dtype=jnp.int32)[:, None]).astype(
        jnp.float32
    )
    local_terms = jnp.einsum(
        "knd,ndr->nkr",
        shaped,
        residual_second[0, 0].astype(jnp.bfloat16),
        preferred_element_type=jnp.float32,
    )
    coarse_residual = jnp.einsum(
        "an,nkr->akr", onehot, local_terms, precision=lax.Precision.HIGHEST
    )
    coarse_rhs = coarse_residual.astype(jnp.bfloat16).reshape((coarse_rows, vectors))
    column_place = lax.axis_index("col") * coarse_rows
    coarse_solution = jnp.dot(
        coarse_inverse,
        lax.all_gather(coarse_rhs, ("row", "col"), axis=0, tiled=True),
        preferred_element_type=jnp.float32,
    )
    coarse_solution = lax.dynamic_slice_in_dim(coarse_solution, column_place, coarse_rows, 0)
    coarse_rounded = coarse_solution.astype(jnp.bfloat16).reshape(
        (aggregates, coarse_dofs, vectors)
    )
    chosen = jnp.einsum(
        "an,akr->nkr",
        onehot.astype(jnp.bfloat16),
        coarse_rounded,
        preferred_element_type=jnp.float32,
    ).astype(jnp.bfloat16)
    correction = jnp.einsum("knd,nkr->ndr", shaped, chosen, preferred_element_type=jnp.float32)[
        None, None
    ]
    after_coarse = second_iter + correction
    residual_third = residual_second - apply_operator(correction)
    return after_coarse + point_smooth(smoother, residual_third)


def solution(mesh):
    placed = (
        P("row", "col", None, None, None),
        P("row", "col", None, None, None),
        P("row", "col", None, None, None),
        P("row", "col", None, None),
        P("row", "col", None, None),
        P("row", "col", None),
        P("row", "col", None, None),
        P("row", None),
    )
    return jax.shard_map(
        body,
        mesh=mesh,
        in_specs=placed,
        out_specs=P("row", "col", None, None, None),
        check_vma=False,
    )
```

profile of v0, /device:TPU:1, one launch (start us, length us, event | category | flops | bytes accessed | tf_op | source)
XLA Modules:
  0.0 296.1 jit_solution(9077023847655563413)
XLA Ops:
  6.5 1.5 compare_and_fusion.1
  9.5 2.9 multiply_add_fusion.8
  14.1 1.4 broadcast_select_fusion.14
  15.5 7.7 %collective-permute-start = (bf16[4,192,128]{2,1,0:T(8,128)(2,1)}, bf16[4,192,128]{2,1,0:T(8,128)(2,1)}, u32[]{:S(2)}, u32[]{:S(2)}) collective-permute-start(bf16[4,192,128]{2,1,0:T(8,128)(2,1)} %broadcast_select_fusion.14), channel_id=1, source_target_pairs={{0,8},{8,16},{16,24},{24,32},{32,40},{40,48},{48,56},{56,64},{64,7... | collective-permute-start | bytes 589832 | tf_op jit(solution)/shard_map/ppermute | solution.py:12
  23.2 1.2 pad_clamp_fusion.3
  25.2 1.4 broadcast_select_fusion.11
  26.6 4.6 %collective-permute-start.1 = (bf16[4,192,128]{2,1,0:T(8,128)(2,1)}, bf16[4,192,128]{2,1,0:T(8,128)(2,1)}, u32[]{:S(2)}, u32[]{:S(2)}) collective-permute-start(bf16[4,192,128]{2,1,0:T(8,128)(2,1)} %broadcast_select_fusion.11), channel_id=1, source_target_pairs={{0,248},{8,0},{16,8},{24,16},{32,24},{40,32},{48,40},{56,48},{64,5... | collective-permute-start | bytes 589832 | tf_op jit(solution)/shard_map/ppermute | solution.py:12
  33.1 1.4 broadcast_select_fusion.8
  34.5 1.6 collective-permute-start.2
  36.1 1.2 pad_clamp_fusion.1
  38.0 1.4 broadcast_select_fusion.5
  39.4 1.4 copy.11
  40.8 1.3 reshape_squeeze.8
  44.4 1.5 reshape_squeeze.9
  47.4 1.6 constant_dynamic-update-slice_fusion.3
  49.0 1.6 constant_dynamic-update-slice_fusion.2
  50.6 1.6 constant_dynamic-update-slice_fusion.1
  52.9 4.8 %gather_fusion.4 = bf16[96,192,128]{2,1,0:T(8,128)(2,1)} fusion(bf16[28,192,128]{2,1,0:T(8,128)(2,1)} %constant_dynamic-update-slice_fusion, s32[1024]{0:T(1024)S(1)} %pad_clamp_fusion), kind=kCustom, calls=%fused_computation.1.clone | custom fusion | bytes 9437568 | tf_op jit(solution)/shard_map/jit(_take)/gather | solution.py:51
  57.8 2.9 broadcast_select_fusion.2
  60.8 5.1 %fusion.15 = f32[1,1,12,192,128]{4,3,2,1,0:T(8,128)S(1)} fusion(f32[1,1,12,192,128]{4,3,2,1,0:T(8,128)S(1)} %copy-done.3, bf16[12,1536,128]{2,1,0:T(8,128)(2,1)S(1)} %bitcast.103, bf16[1,1,12,192,1536]{4,3,2,1,0:T(8,128)(2,1)} %param.14), kind=kOutput, calls=%fused_computation.28 | convolution fusion | flops 906264576 | bytes 14155776 | tf_op jit(solution)/shard_map/nde,ner->ndr/dot_general | solution.py:52
  65.9 1.2 multiply_add_fusion.5
  67.4 1.3 fusion.25
  68.7 1.4 gather_fusion.8
  76.5 8.7 %collective-permute-start.5 = (bf16[4,192,128]{2,1,0:T(8,128)(2,1)S(1)}, bf16[4,192,128]{2,1,0:T(8,128)(2,1)S(1)}, u32[]{:S(2)}, u32[]{:S(2)}) collective-permute-start(bf16[4,192,128]{2,1,0:T(8,128)(2,1)S(1)} %broadcast_select_fusion.10), channel_id=1, source_target_pairs={{0,248},{8,0},{16,8},{24,16},{32,24},{40,32},{48,40},{56,48},{64,5... | collective-permute-start | bytes 589832 | tf_op jit(solution)/shard_map/ppermute | solution.py:12
  85.2 2.3 collective-permute-start.6
  87.5 1.2 collective-permute-start.7
  91.4 5.1 %collective-permute-done.6 = bf16[4,192,128]{2,1,0:T(8,128)(2,1)S(1)} collective-permute-done((bf16[4,192,128]{2,1,0:T(8,128)(2,1)S(1)}, bf16[4,192,128]{2,1,0:T(8,128)(2,1)S(1)}, u32[]{:S(2)}, u32[]{:S(2)}) %collective-permute-start.6) | collective-permute-done | bytes 196640 | tf_op jit(solution)/shard_map/ppermute | solution.py:12
  97.2 3.3 %collective-permute-done.7 = bf16[4,192,128]{2,1,0:T(8,128)(2,1)S(1)} collective-permute-done((bf16[4,192,128]{2,1,0:T(8,128)(2,1)S(1)}, bf16[4,192,128]{2,1,0:T(8,128)(2,1)S(1)}, u32[]{:S(2)}, u32[]{:S(2)}) %collective-permute-start.7) | collective-permute-done | bytes 196640 | tf_op jit(solution)/shard_map/ppermute | solution.py:12
  101.3 5.0 %gather_fusion.9 = bf16[96,192,128]{2,1,0:T(8,128)(2,1)} fusion(bf16[28,192,128]{2,1,0:T(8,128)(2,1)} %constant_dynamic-update-slice_fusion.5, s32[1024]{0:T(1024)} %copy-done.32), kind=kCustom, calls=%fused_computation.13.clone | custom fusion | bytes 9437568 | tf_op jit(solution)/shard_map/jit(_take)/gather | solution.py:51
  106.2 2.9 broadcast_select_fusion.1
  109.2 5.0 %fusion.18 = f32[1,1,12,192,128]{4,3,2,1,0:T(8,128)S(1)} fusion(f32[1,1,12,192,128]{4,3,2,1,0:T(8,128)S(1)} %copy-done.2, bf16[12,1536,128]{2,1,0:T(8,128)(2,1)S(1)} %bitcast.102, bf16[1,1,12,192,1536]{4,3,2,1,0:T(8,128)(2,1)} %param.14), kind=kOutput, calls=%fused_computation.29 | convolution fusion | flops 906264576 | bytes 14155776 | tf_op jit(solution)/shard_map/nde,ner->ndr/dot_general | solution.py:52
  115.2 1.3 reshape.213
  116.5 102.9 %all-gather.2.cloned.1.call-done = bf16[6144,128]{1,0:T(8,128)(2,1)} async-done(((bf16[24,128]{1,0:T(8,128)(2,1)}), bf16[6144,128]{1,0:T(8,128)(2,1)}) %all-gather.2.cloned.1.call-update) | async-done | bytes 1572880 | tf_op jit(solution)/shard_map/all_gather | solution.py:80
  219.5 2.2 fusion.43
  222.3 1.3 reshape.214
  224.5 2.6 constant_dynamic-update-slice_fusion.14
  227.1 2.4 gather_fusion.13
  229.5 2.4 gather_fusion.12
  232.0 2.4 gather_fusion.11
  234.4 2.5 gather_fusion.10
  239.9 7.6 %collective-permute-start.9 = (bf16[4,192,128]{2,1,0:T(8,128)(2,1)S(1)}, bf16[4,192,128]{2,1,0:T(8,128)(2,1)S(1)}, u32[]{:S(2)}, u32[]{:S(2)}) collective-permute-start(bf16[4,192,128]{2,1,0:T(8,128)(2,1)S(1)} %broadcast_select_fusion.9), channel_id=1, source_target_pairs={{0,248},{8,0},{16,8},{24,16},{32,24},{40,32},{48,40},{56,48},{64,5... | collective-permute-start | bytes 589832 | tf_op jit(solution)/shard_map/ppermute | solution.py:12
  248.5 1.7 collective-permute-start.10
  250.2 19.2 %collective-permute-done.8 = bf16[4,192,128]{2,1,0:T(8,128)(2,1)S(1)} collective-permute-done((bf16[4,192,128]{2,1,0:T(8,128)(2,1)S(1)}, bf16[4,192,128]{2,1,0:T(8,128)(2,1)S(1)}, u32[]{:S(2)}, u32[]{:S(2)}) %collective-permute-start.8) | collective-permute-done | bytes 196640 | tf_op jit(solution)/shard_map/ppermute | solution.py:12
  272.3 5.0 %gather_fusion.14 = bf16[96,192,128]{2,1,0:T(8,128)(2,1)} fusion(bf16[28,192,128]{2,1,0:T(8,128)(2,1)} %constant_dynamic-update-slice_fusion.10, s32[1024]{0:T(1024)} %copy-done.32), kind=kCustom, calls=%fused_computation.14.clone | custom fusion | bytes 9437568 | tf_op jit(solution)/shard_map/jit(_take)/gather | solution.py:51
  277.2 2.8 broadcast_select_fusion
  280.1 5.1 %fusion.21 = f32[1,1,12,192,128]{4,3,2,1,0:T(8,128)S(1)} fusion(f32[1,1,12,192,128]{4,3,2,1,0:T(8,128)S(1)} %fusion.18, bf16[12,1536,128]{2,1,0:T(8,128)(2,1)S(1)} %bitcast.101, bf16[1,1,12,192,1536]{4,3,2,1,0:T(8,128)(2,1)} %param.14), kind=kOutput, calls=%fused_computation.30 | convolution fusion | flops 906264576 | bytes 14155776 | tf_op jit(solution)/shard_map/nde,ner->ndr/dot_general | solution.py:52
  285.2 1.2 multiply_add_fusion.2
  288.1 1.2 add_bitcast_fusion
  (127 shorter events, 32.7 us)
Async XLA Ops:
  6.5 213.0 %copy-start = (bf16[192,6144]{1,0:T(8,128)(2,1)S(1)}, bf16[192,6144]{1,0:T(8,128)(2,1)}, u32[]{:S(2)}) copy-start(bf16[192,6144]{1,0:T(8,128)(2,1)} %param.19) | copy-start | bytes 7077892
  6.5 212.9 %all-gather.2.cloned.1.call-start = ((), (), s32[]{:S(2)}) async-start(), calls=%async_computation | async-start | bytes 1579008 | tf_op jit(solution)/shard_map/all_gather | solution.py:80
  9.4 3.9 %copy-start.11 = (f32[12,64]{1,0:T(8,128)}, f32[12,64]{1,0:T(8,128)S(1)}, u32[]{:S(2)}) copy-start(f32[12,64]{1,0:T(8,128)S(1)} %get-tuple-element.30) | copy-start | bytes 9220
  9.5 3.9 %copy-start.14 = (f32[12,64]{1,0:T(8,128)}, f32[12,64]{1,0:T(8,128)S(1)}, u32[]{:S(2)}) copy-start(f32[12,64]{1,0:T(8,128)S(1)} %get-tuple-element.31) | copy-start | bytes 9220
  9.5 3.9 %copy-start.17 = (f32[12,64]{1,0:T(8,128)}, f32[12,64]{1,0:T(8,128)S(1)}, u32[]{:S(2)}) copy-start(f32[12,64]{1,0:T(8,128)S(1)} %get-tuple-element.32) | copy-start | bytes 9220
  9.5 3.9 %copy-start.20 = (f32[12,64]{1,0:T(8,128)}, f32[12,64]{1,0:T(8,128)S(1)}, u32[]{:S(2)}) copy-start(f32[12,64]{1,0:T(8,128)S(1)} %get-tuple-element.33) | copy-start | bytes 9220
  9.5 3.9 %copy-start.23 = (f32[12,64]{1,0:T(8,128)}, f32[12,64]{1,0:T(8,128)S(1)}, u32[]{:S(2)}) copy-start(f32[12,64]{1,0:T(8,128)S(1)} %get-tuple-element.34) | copy-start | bytes 9220
  9.5 3.9 %copy-start.26 = (f32[12,64]{1,0:T(8,128)}, f32[12,64]{1,0:T(8,128)S(1)}, u32[]{:S(2)}) copy-start(f32[12,64]{1,0:T(8,128)S(1)} %get-tuple-element.35) | copy-start | bytes 9220
  9.5 3.9 %copy-start.29 = (f32[12,64]{1,0:T(8,128)}, f32[12,64]{1,0:T(8,128)S(1)}, u32[]{:S(2)}) copy-start(f32[12,64]{1,0:T(8,128)S(1)} %get-tuple-element.36) | copy-start | bytes 9220
  12.4 1.0 copy-start.8
  15.5 31.9 %collective-permute-start = (bf16[4,192,128]{2,1,0:T(8,128)(2,1)}, bf16[4,192,128]{2,1,0:T(8,128)(2,1)}, u32[]{:S(2)}, u32[]{:S(2)}) collective-permute-start(bf16[4,192,128]{2,1,0:T(8,128)(2,1)} %broadcast_select_fusion.14), channel_id=1, source_target_pairs={{0,8},{8,16},{16,24},{24,32},{32,40},{40,48},{48,56},{56,64},{64,7... | collective-permute-start | bytes 589832 | tf_op jit(solution)/shard_map/ppermute | solution.py:12
  26.6 22.4 %collective-permute-start.1 = (bf16[4,192,128]{2,1,0:T(8,128)(2,1)}, bf16[4,192,128]{2,1,0:T(8,128)(2,1)}, u32[]{:S(2)}, u32[]{:S(2)}) collective-permute-start(bf16[4,192,128]{2,1,0:T(8,128)(2,1)} %broadcast_select_fusion.11), channel_id=1, source_target_pairs={{0,248},{8,0},{16,8},{24,16},{32,24},{40,32},{48,40},{56,48},{64,5... | collective-permute-start | bytes 589832 | tf_op jit(solution)/shard_map/ppermute | solution.py:12
  34.5 16.1 %collective-permute-start.2 = (bf16[4,192,128]{2,1,0:T(8,128)(2,1)}, bf16[4,192,128]{2,1,0:T(8,128)(2,1)}, u32[]{:S(2)}, u32[]{:S(2)}) collective-permute-start(bf16[4,192,128]{2,1,0:T(8,128)(2,1)} %broadcast_select_fusion.8), channel_id=1, source_target_pairs={{0,1},{1,2},{2,3},{3,4},{4,5},{5,6},{6,7},{7,0},{8,9},{9,10},{10,1... | collective-permute-start | bytes 589832 | tf_op jit(solution)/shard_map/ppermute | solution.py:12
  39.4 12.8 %collective-permute-start.3 = (bf16[4,192,128]{2,1,0:T(8,128)(2,1)}, bf16[4,192,128]{2,1,0:T(8,128)(2,1)S(1)}, u32[]{:S(2)}, u32[]{:S(2)}) collective-permute-start(bf16[4,192,128]{2,1,0:T(8,128)(2,1)} %broadcast_select_fusion.5), channel_id=1, source_target_pairs={{0,7},{1,0},{2,1},{3,2},{4,3},{5,4},{6,5},{7,6},{8,15},{9,8},{10,9... | collective-permute-start | bytes 589832 | tf_op jit(solution)/shard_map/ppermute | solution.py:12
  47.4 10.4 %copy-start.32 = (s32[1024]{0:T(1024)}, s32[1024]{0:T(1024)S(1)}, u32[]{:S(2)}) copy-start(s32[1024]{0:T(1024)S(1)} %pad_clamp_fusion) | copy-start | bytes 12292
  52.9 4.8 %copy-start.33 = (pred[96]{0:T(512)(128)(4,1)S(1)}, pred[96]{0:T(512)(128)(4,1)}, u32[]{:S(2)}) copy-start(pred[96]{0:T(512)(128)(4,1)} %compare_and_fusion) | copy-start | bytes 292
  57.8 2.9 copy-start.3
  60.7 5.2 %copy-start.12 = (f32[12,64]{1,0:T(8,128)S(1)}, f32[12,64]{1,0:T(8,128)}, u32[]{:S(2)}) copy-start(f32[12,64]{1,0:T(8,128)} %copy-done.11) | copy-start | bytes 9220
  60.7 5.2 %copy-start.15 = (f32[12,64]{1,0:T(8,128)S(1)}, f32[12,64]{1,0:T(8,128)}, u32[]{:S(2)}) copy-start(f32[12,64]{1,0:T(8,128)} %copy-done.14) | copy-start | bytes 9220
  60.7 5.2 %copy-start.18 = (f32[12,64]{1,0:T(8,128)S(1)}, f32[12,64]{1,0:T(8,128)}, u32[]{:S(2)}) copy-start(f32[12,64]{1,0:T(8,128)} %copy-done.17) | copy-start | bytes 9220
  60.7 5.2 %copy-start.21 = (f32[12,64]{1,0:T(8,128)S(1)}, f32[12,64]{1,0:T(8,128)}, u32[]{:S(2)}) copy-start(f32[12,64]{1,0:T(8,128)} %copy-done.20) | copy-start | bytes 9220
  60.8 5.2 %copy-start.24 = (f32[12,64]{1,0:T(8,128)S(1)}, f32[12,64]{1,0:T(8,128)}, u32[]{:S(2)}) copy-start(f32[12,64]{1,0:T(8,128)} %copy-done.23) | copy-start | bytes 9220
  60.8 5.2 %copy-start.27 = (f32[12,64]{1,0:T(8,128)S(1)}, f32[12,64]{1,0:T(8,128)}, u32[]{:S(2)}) copy-start(f32[12,64]{1,0:T(8,128)} %copy-done.26) | copy-start | bytes 9220
  60.8 5.2 %copy-start.30 = (f32[12,64]{1,0:T(8,128)S(1)}, f32[12,64]{1,0:T(8,128)}, u32[]{:S(2)}) copy-start(f32[12,64]{1,0:T(8,128)} %copy-done.29) | copy-start | bytes 9220
  65.8 2.9 copy-start.1
  65.9 1.3 copy-start.7
  65.9 1.5 copy-start.9
  74.7 14.9 %collective-permute-start.4 = (bf16[4,192,128]{2,1,0:T(8,128)(2,1)S(1)}, bf16[4,192,128]{2,1,0:T(8,128)(2,1)S(1)}, u32[]{:S(2)}, u32[]{:S(2)}) collective-permute-start(bf16[4,192,128]{2,1,0:T(8,128)(2,1)S(1)} %broadcast_select_fusion.13), channel_id=1, source_target_pairs={{0,8},{8,16},{16,24},{24,32},{32,40},{40,48},{48,56},{56,64},{64,7... | collective-permute-start | bytes 589832 | tf_op jit(solution)/shard_map/ppermute | solution.py:12
  76.5 14.2 %collective-permute-start.5 = (bf16[4,192,128]{2,1,0:T(8,128)(2,1)S(1)}, bf16[4,192,128]{2,1,0:T(8,128)(2,1)S(1)}, u32[]{:S(2)}, u32[]{:S(2)}) collective-permute-start(bf16[4,192,128]{2,1,0:T(8,128)(2,1)S(1)} %broadcast_select_fusion.10), channel_id=1, source_target_pairs={{0,248},{8,0},{16,8},{24,16},{32,24},{40,32},{48,40},{56,48},{64,5... | collective-permute-start | bytes 589832 | tf_op jit(solution)/shard_map/ppermute | solution.py:12
  85.2 11.4 %collective-permute-start.6 = (bf16[4,192,128]{2,1,0:T(8,128)(2,1)S(1)}, bf16[4,192,128]{2,1,0:T(8,128)(2,1)S(1)}, u32[]{:S(2)}, u32[]{:S(2)}) collective-permute-start(bf16[4,192,128]{2,1,0:T(8,128)(2,1)S(1)} %broadcast_select_fusion.7), channel_id=1, source_target_pairs={{0,1},{1,2},{2,3},{3,4},{4,5},{5,6},{6,7},{7,0},{8,9},{9,10},{10,1... | collective-permute-start | bytes 589832 | tf_op jit(solution)/shard_map/ppermute | solution.py:12
  87.5 13.1 %collective-permute-start.7 = (bf16[4,192,128]{2,1,0:T(8,128)(2,1)S(1)}, bf16[4,192,128]{2,1,0:T(8,128)(2,1)S(1)}, u32[]{:S(2)}, u32[]{:S(2)}) collective-permute-start(bf16[4,192,128]{2,1,0:T(8,128)(2,1)S(1)} %broadcast_select_fusion.4), channel_id=1, source_target_pairs={{0,7},{1,0},{2,1},{3,2},{4,3},{5,4},{6,5},{7,6},{8,15},{9,8},{10,9... | collective-permute-start | bytes 589832 | tf_op jit(solution)/shard_map/ppermute | solution.py:12
  101.3 5.0 %copy-start.34 = (pred[96]{0:T(512)(128)(4,1)S(1)}, pred[96]{0:T(512)(128)(4,1)}, u32[]{:S(2)}) copy-start(pred[96]{0:T(512)(128)(4,1)} %compare_and_fusion) | copy-start | bytes 292
  106.2 2.9 copy-start.2
  109.2 5.0 %copy-start.10 = (bf16[6,12,192]{2,1,0:T(8,128)(2,1)S(1)}, bf16[6,12,192]{2,1,0:T(8,128)(2,1)}, u32[]{:S(2)}) copy-start(bf16[6,12,192]{2,1,0:T(8,128)(2,1)} %reshape_squeeze.9) | copy-start | bytes 82948
  109.2 5.3 %copy-start.35 = (s32[1,1,12]{2,1,0:T(1,128)S(1)}, s32[1,1,12]{2,1,0:T(1,128)}, u32[]{:S(2)}) copy-start(s32[1,1,12]{2,1,0:T(1,128)} %param.17) | copy-start | bytes 148
  239.9 30.3 %collective-permute-start.9 = (bf16[4,192,128]{2,1,0:T(8,128)(2,1)S(1)}, bf16[4,192,128]{2,1,0:T(8,128)(2,1)S(1)}, u32[]{:S(2)}, u32[]{:S(2)}) collective-permute-start(bf16[4,192,128]{2,1,0:T(8,128)(2,1)S(1)} %broadcast_select_fusion.9), channel_id=1, source_target_pairs={{0,248},{8,0},{16,8},{24,16},{32,24},{40,32},{48,40},{56,48},{64,5... | collective-permute-start | bytes 589832 | tf_op jit(solution)/shard_map/ppermute | solution.py:12
  247.5 22.0 %collective-permute-start.8 = (bf16[4,192,128]{2,1,0:T(8,128)(2,1)S(1)}, bf16[4,192,128]{2,1,0:T(8,128)(2,1)S(1)}, u32[]{:S(2)}, u32[]{:S(2)}) collective-permute-start(bf16[4,192,128]{2,1,0:T(8,128)(2,1)S(1)} %broadcast_select_fusion.12), channel_id=1, source_target_pairs={{0,8},{8,16},{16,24},{24,32},{32,40},{40,48},{48,56},{56,64},{64,7... | collective-permute-start | bytes 589832 | tf_op jit(solution)/shard_map/ppermute | solution.py:12
  248.5 22.3 %collective-permute-start.10 = (bf16[4,192,128]{2,1,0:T(8,128)(2,1)S(1)}, bf16[4,192,128]{2,1,0:T(8,128)(2,1)S(1)}, u32[]{:S(2)}, u32[]{:S(2)}) collective-permute-start(bf16[4,192,128]{2,1,0:T(8,128)(2,1)S(1)} %broadcast_select_fusion.6), channel_id=1, source_target_pairs={{0,1},{1,2},{2,3},{3,4},{4,5},{5,6},{6,7},{7,0},{8,9},{9,10},{10,1... | collective-permute-start | bytes 589832 | tf_op jit(solution)/shard_map/ppermute | solution.py:12
  250.2 21.3 %collective-permute-start.11 = (bf16[4,192,128]{2,1,0:T(8,128)(2,1)S(1)}, bf16[4,192,128]{2,1,0:T(8,128)(2,1)S(1)}, u32[]{:S(2)}, u32[]{:S(2)}) collective-permute-start(bf16[4,192,128]{2,1,0:T(8,128)(2,1)S(1)} %broadcast_select_fusion.3), channel_id=1, source_target_pairs={{0,7},{1,0},{2,1},{3,2},{4,3},{5,4},{6,5},{7,6},{8,15},{9,8},{10,9... | collective-permute-start | bytes 589832 | tf_op jit(solution)/shard_map/ppermute | solution.py:12
  280.0 5.1 %copy-start.13 = (f32[12,64]{1,0:T(8,128)S(1)}, f32[12,64]{1,0:T(8,128)}, u32[]{:S(2)}) copy-start(f32[12,64]{1,0:T(8,128)} %copy-done.11) | copy-start | bytes 9220
  280.1 5.1 %copy-start.16 = (f32[12,64]{1,0:T(8,128)S(1)}, f32[12,64]{1,0:T(8,128)}, u32[]{:S(2)}) copy-start(f32[12,64]{1,0:T(8,128)} %copy-done.14) | copy-start | bytes 9220
  280.1 5.1 %copy-start.19 = (f32[12,64]{1,0:T(8,128)S(1)}, f32[12,64]{1,0:T(8,128)}, u32[]{:S(2)}) copy-start(f32[12,64]{1,0:T(8,128)} %copy-done.17) | copy-start | bytes 9220
  280.1 5.1 %copy-start.22 = (f32[12,64]{1,0:T(8,128)S(1)}, f32[12,64]{1,0:T(8,128)}, u32[]{:S(2)}) copy-start(f32[12,64]{1,0:T(8,128)} %copy-done.20) | copy-start | bytes 9220
  280.1 5.1 %copy-start.25 = (f32[12,64]{1,0:T(8,128)S(1)}, f32[12,64]{1,0:T(8,128)}, u32[]{:S(2)}) copy-start(f32[12,64]{1,0:T(8,128)} %copy-done.23) | copy-start | bytes 9220
  280.1 5.1 %copy-start.28 = (f32[12,64]{1,0:T(8,128)S(1)}, f32[12,64]{1,0:T(8,128)}, u32[]{:S(2)}) copy-start(f32[12,64]{1,0:T(8,128)} %copy-done.26) | copy-start | bytes 9220
  280.1 5.1 %copy-start.31 = (f32[12,64]{1,0:T(8,128)S(1)}, f32[12,64]{1,0:T(8,128)}, u32[]{:S(2)}) copy-start(f32[12,64]{1,0:T(8,128)} %copy-done.29) | copy-start | bytes 9220
  286.5 1.3 copy-start.4
  286.5 1.6 copy-start.5
  (1 other events, 0.7 us)
Sparse Core Ops, SparseCore 0:
  116.7 102.7 all-gather.1
where the time goes:
time: 297 us; the launch traced here: 296 us
  waiting for transfers between devices  131 us (44%)
  local copies, waits for them, and re-layouts  54.9 us (18%)
  other arithmetic  38.2 us (13%)
  starting transfers between devices  36.5 us (12%)
  matrix products  21.3 us (7%)
  between operations  14.1 us (5%)
    all_gather x1, waiting for transfers between devices, body(): lax.all_gather(coarse_rhs, ('row', 'col'), axis=0, tiled=True)  103 us
    ppermute x12, starting transfers between devices, passed_along(): return lax.ppermute(value, axis, pairs)  36.5 us
    ppermute x12, waiting for transfers between devices, passed_along(): return lax.ppermute(value, axis, pairs)  28.2 us
    dot_general x3, matrix products, apply_operator(): jnp.einsum('nde,ner->ndr', blocks[0, 0], picked, preferred_element_type=j...  15.1 us
    gather x3, local copies, waits for them, and re-layouts, apply_operator(): jnp.take(source, columns.reshape(-1), axis=0)  14.7 us
    unnamed x84, local copies, waits for them, and re-layouts  14.6 us
    select_n x4, other arithmetic, apply_operator(): jnp.take(source, columns.reshape(-1), axis=0)  9.78 us
    gather x6, local copies, waits for them, and re-layouts, apply_operator(): packed = jnp.take(shard_low, send_rows[2 if offset == 1 else 3], axis=0)  8.34 us
  transfers between devices with their start and end apart: 13, of which 5 were waited for; matrix products, arithmetic and copies ran while one was open for 10% of the time, Pallas kernels for 0%

commit v1 on v0

--- a/solution.py
+++ b/solution.py
@@ -4,6 +4,15 @@
 from jax.sharding import PartitionSpec as P
 
 damping = 0.6
+
+
+def state_the_sources_all(local_values):
+    return jnp.concatenate(
+        lax.all_to_all(
+            jnp.stack(lax.axis_size(("row", "col")) * [local_values], 0), ("row", "col"), 0, 0
+        ),
+        0,
+    )
 
 
 def passed_along(value, axis, steps):
@@ -76,9 +85,7 @@
     coarse_rhs = coarse_residual.astype(jnp.bfloat16).reshape((coarse_rows, vectors))
     column_place = lax.axis_index("col") * coarse_rows
     coarse_solution = jnp.dot(
-        coarse_inverse,
-        lax.all_gather(coarse_rhs, ("row", "col"), axis=0, tiled=True),
-        preferred_element_type=jnp.float32,
+        coarse_inverse, state_the_sources_all(coarse_rhs), preferred_element_type=jnp.float32
     )
     coarse_solution = lax.dynamic_slice_in_dim(coarse_solution, column_place, coarse_rows, 0)
     coarse_rounded = coarse_solution.astype(jnp.bfloat16).reshape(

time: 297 us -> 231 us (0.78)
  waiting for transfers between devices: 131 us -> 67.3 us
  between operations: 14.1 us -> 0.69 us
  starting transfers between devices: 36.5 us -> 45.3 us
    all_gather x1 -> x0, waiting for transfers between devices: 103 us -> none  [body(): lax.all_gather(coarse_rhs, ('row', 'col'), axis=0, tiled=True)]
    all_to_all x0 -> x1, waiting for transfers between devices: none -> 42.9 us  [state_the_sources_all(): lax.all_to_all(jnp.stack(lax.axis_size(('row', 'col')) * [local_values],...]
    all_to_all x0 -> x1, starting transfers between devices: none -> 12.1 us  [state_the_sources_all(): lax.all_to_all(jnp.stack(lax.axis_size(('row', 'col')) * [local_values],...]
    ppermute x12, waiting for transfers between devices: 28.2 us -> 24.4 us  [passed_along(): return lax.ppermute(value, axis, pairs)]
    another operation x0 -> x2, local copies, waits for them, and re-layouts: none -> 3.37 us  [state_the_sources_all(): jnp.stack(lax.axis_size(('row', 'col')) * [local_values], 0)]
    ppermute x12, starting transfers between devices: 36.5 us -> 33.2 us  [passed_along(): return lax.ppermute(value, axis, pairs)]
  transfers between devices with their start and end apart: 13 -> 13, of which waited for: 5 -> 7; matrix products, arithmetic and copies ran while one was open for 10% -> 13% of each run, Pallas kernels for 0% -> 0%
where the time goes in v1:
time: 231 us; the launch traced here: 230 us
  waiting for transfers between devices  67.3 us (29%)
  local copies, waits for them, and re-layouts  57 us (25%)
  starting transfers between devices  45.3 us (20%)
  other arithmetic  38 us (16%)
  matrix products  21.3 us (9%)
    all_to_all x1, waiting for transfers between devices, state_the_sources_all(): lax.all_to_all(jnp.stack(lax.axis_size(('row', 'col')) * [local_values],...  42.9 us
    ppermute x12, starting transfers between devices, passed_along(): return lax.ppermute(value, axis, pairs)  33.2 us
    ppermute x12, waiting for transfers between devices, passed_along(): return lax.ppermute(value, axis, pairs)  24.4 us
    dot_general x3, matrix products, apply_operator(): jnp.einsum('nde,ner->ndr', blocks[0, 0], picked, preferred_element_type=j...  15.1 us
    gather x3, local copies, waits for them, and re-layouts, apply_operator(): jnp.take(source, columns.reshape(-1), axis=0)  14.8 us
    unnamed x84, local copies, waits for them, and re-layouts  14.7 us
    all_to_all x1, starting transfers between devices, state_the_sources_all(): lax.all_to_all(jnp.stack(lax.axis_size(('row', 'col')) * [local_values],...  12.1 us
    select_n x4, other arithmetic, apply_operator(): jnp.take(source, columns.reshape(-1), axis=0)  9.71 us
  transfers between devices with their start and end apart: 13, of which 7 were waited for; matrix products, arithmetic and copies ran while one was open for 13% of the time, Pallas kernels for 0%

profile of v1, /device:TPU:1, one launch (start us, length us, event | category | flops | bytes accessed | tf_op | source)
XLA Modules:
  0.0 229.6 jit_solution(2443327972444680252)
XLA Ops:
  0.0 1.5 compare_and_fusion.1
  3.0 2.9 %multiply_add_fusion.8 = (f32[1,1,12,1,64,128]{5,4,3,2,1,0:T(8,128)S(1)}, f32[1,1,12,1,64,128]{5,4,3,2,1,0:T(8,128)S(1)}, f32[1,1,12,1,64,128]{5,4,3,2,1,0:T(8,128)S(1)}) fusion(f32[1,1,12,3,64,128]{5,4,3,2,1,0:T(8,128)} %bitcast.106, f32[12,64]{1,0:T(8,128)S(1)} %get-tuple-element.35, f32[12,64]{1,0:T(8,128)S(1)} %get-tuple-element.36, ...), kind=kLoop, calls=%fused_computation.50 | loop fusion | flops 1474560 | bytes 2386944 | tf_op jit(solution)/shard_map/add | solution.py:35
  7.6 1.4 broadcast_select_fusion.14
  9.0 7.7 %collective-permute-start = (bf16[4,192,128]{2,1,0:T(8,128)(2,1)}, bf16[4,192,128]{2,1,0:T(8,128)(2,1)}, u32[]{:S(2)}, u32[]{:S(2)}) collective-permute-start(bf16[4,192,128]{2,1,0:T(8,128)(2,1)} %broadcast_select_fusion.14), channel_id=1, source_target_pairs={{0,8},{8,16},{16,24},{24,32},{32,40},{40,48},{48,56},{56,64},{64,7... | collective-permute-start | bytes 589832 | tf_op jit(solution)/shard_map/ppermute | solution.py:21
  16.7 1.2 pad_clamp_fusion.3
  18.7 1.4 broadcast_select_fusion.11
  20.1 4.6 %collective-permute-start.1 = (bf16[4,192,128]{2,1,0:T(8,128)(2,1)}, bf16[4,192,128]{2,1,0:T(8,128)(2,1)}, u32[]{:S(2)}, u32[]{:S(2)}) collective-permute-start(bf16[4,192,128]{2,1,0:T(8,128)(2,1)} %broadcast_select_fusion.11), channel_id=1, source_target_pairs={{0,248},{8,0},{16,8},{24,16},{32,24},{40,32},{48,40},{56,48},{64,5... | collective-permute-start | bytes 589832 | tf_op jit(solution)/shard_map/ppermute | solution.py:21
  24.7 1.2 pad_clamp_fusion.2
  26.6 1.3 broadcast_select_fusion.8
  28.0 1.6 collective-permute-start.2
  31.4 1.4 broadcast_select_fusion.5
  32.8 1.4 copy.11
  34.2 1.3 reshape_squeeze.8
  37.7 1.5 reshape_squeeze.9
  40.6 1.6 constant_dynamic-update-slice_fusion.3
  42.2 1.6 constant_dynamic-update-slice_fusion.2
  43.9 1.6 constant_dynamic-update-slice_fusion.1
  46.2 4.8 %gather_fusion.4 = bf16[96,192,128]{2,1,0:T(8,128)(2,1)} fusion(bf16[28,192,128]{2,1,0:T(8,128)(2,1)} %constant_dynamic-update-slice_fusion, s32[1024]{0:T(1024)S(1)} %pad_clamp_fusion), kind=kCustom, calls=%fused_computation.1.clone | custom fusion | bytes 9437568 | tf_op jit(solution)/shard_map/jit(_take)/gather | solution.py:60
  51.0 2.9 %broadcast_select_fusion.2 = bf16[96,192,128]{2,1,0:T(8,128)(2,1)S(1)} fusion(bf16[96,192,128]{2,1,0:T(8,128)(2,1)} %gather_fusion.4, pred[96]{0:T(512)(128)(4,1)S(1)} %copy-done.33), kind=kLoop, calls=%fused_computation.23 | loop fusion | flops 2359296 | bytes 9437280 | tf_op jit(solution)/shard_map/jit(_take)/select_n | solution.py:60
  54.0 5.1 %fusion.15 = f32[1,1,12,192,128]{4,3,2,1,0:T(8,128)S(1)} fusion(f32[1,1,12,192,128]{4,3,2,1,0:T(8,128)S(1)} %copy-done.3, bf16[12,1536,128]{2,1,0:T(8,128)(2,1)S(1)} %bitcast.104, bf16[1,1,12,192,1536]{4,3,2,1,0:T(8,128)(2,1)} %param.14), kind=kOutput, calls=%fused_computation.28 | convolution fusion | flops 906264576 | bytes 14155776 | tf_op jit(solution)/shard_map/nde,ner->ndr/dot_general | solution.py:61
  60.6 1.3 fusion.25
  61.9 1.4 gather_fusion.8
  69.7 8.7 %collective-permute-start.5 = (bf16[4,192,128]{2,1,0:T(8,128)(2,1)S(1)}, bf16[4,192,128]{2,1,0:T(8,128)(2,1)S(1)}, u32[]{:S(2)}, u32[]{:S(2)}) collective-permute-start(bf16[4,192,128]{2,1,0:T(8,128)(2,1)S(1)} %broadcast_select_fusion.10), channel_id=1, source_target_pairs={{0,248},{8,0},{16,8},{24,16},{32,24},{40,32},{48,40},{56,48},{64,5... | collective-permute-start | bytes 589832 | tf_op jit(solution)/shard_map/ppermute | solution.py:21
  78.4 2.3 %collective-permute-start.6 = (bf16[4,192,128]{2,1,0:T(8,128)(2,1)S(1)}, bf16[4,192,128]{2,1,0:T(8,128)(2,1)S(1)}, u32[]{:S(2)}, u32[]{:S(2)}) collective-permute-start(bf16[4,192,128]{2,1,0:T(8,128)(2,1)S(1)} %broadcast_select_fusion.7), channel_id=1, source_target_pairs={{0,1},{1,2},{2,3},{3,4},{4,5},{5,6},{6,7},{7,0},{8,9},{9,10},{10,1... | collective-permute-start | bytes 589832 | tf_op jit(solution)/shard_map/ppermute | solution.py:21
  84.6 5.1 %collective-permute-done.6 = bf16[4,192,128]{2,1,0:T(8,128)(2,1)S(1)} collective-permute-done((bf16[4,192,128]{2,1,0:T(8,128)(2,1)S(1)}, bf16[4,192,128]{2,1,0:T(8,128)(2,1)S(1)}, u32[]{:S(2)}, u32[]{:S(2)}) %collective-permute-start.6) | collective-permute-done | bytes 196640 | tf_op jit(solution)/shard_map/ppermute | solution.py:21
  90.5 3.3 %collective-permute-done.7 = bf16[4,192,128]{2,1,0:T(8,128)(2,1)S(1)} collective-permute-done((bf16[4,192,128]{2,1,0:T(8,128)(2,1)S(1)}, bf16[4,192,128]{2,1,0:T(8,128)(2,1)S(1)}, u32[]{:S(2)}, u32[]{:S(2)}) %collective-permute-start.7) | collective-permute-done | bytes 196640 | tf_op jit(solution)/shard_map/ppermute | solution.py:21
  94.4 5.0 %gather_fusion.9 = bf16[96,192,128]{2,1,0:T(8,128)(2,1)} fusion(bf16[28,192,128]{2,1,0:T(8,128)(2,1)} %constant_dynamic-update-slice_fusion.5, s32[1024]{0:T(1024)} %copy-done.32), kind=kCustom, calls=%fused_computation.13.clone | custom fusion | bytes 9437568 | tf_op jit(solution)/shard_map/jit(_take)/gather | solution.py:60
  99.4 2.9 %broadcast_select_fusion.1 = bf16[96,192,128]{2,1,0:T(8,128)(2,1)S(1)} fusion(bf16[96,192,128]{2,1,0:T(8,128)(2,1)} %gather_fusion.9, pred[96]{0:T(512)(128)(4,1)S(1)} %copy-done.34), kind=kLoop, calls=%fused_computation.22 | loop fusion | flops 2359296 | bytes 9437280 | tf_op jit(solution)/shard_map/jit(_take)/select_n | solution.py:60
  102.4 5.0 %fusion.18 = f32[1,1,12,192,128]{4,3,2,1,0:T(8,128)S(1)} fusion(f32[1,1,12,192,128]{4,3,2,1,0:T(8,128)S(1)} %copy-done.2, bf16[12,1536,128]{2,1,0:T(8,128)(2,1)S(1)} %bitcast.103, bf16[1,1,12,192,1536]{4,3,2,1,0:T(8,128)(2,1)} %param.14), kind=kOutput, calls=%fused_computation.29 | convolution fusion | flops 906264576 | bytes 14155776 | tf_op jit(solution)/shard_map/nde,ner->ndr/dot_general | solution.py:61
  108.4 1.3 stack_reshape.2
  109.7 2.1 stack.10
  111.8 12.1 %all-to-all-start = ((bf16[256,24,128]{2,1,0:T(8,128)(2,1)}), bf16[256,24,128]{2,1,0:T(8,128)(2,1)}, u32[]{:S(2)}, u32[]{:S(2)}) async-start(bf16[256,24,128]{2,1,0:T(8,128)(2,1)} %stack.10), calls=%async_computation | async-start | bytes 3145728 | tf_op jit(solution)/shard_map/all_to_all | solution.py:11
  123.9 42.9 %all-to-all-done = bf16[256,24,128]{2,1,0:T(8,128)(2,1)} async-done(((bf16[256,24,128]{2,1,0:T(8,128)(2,1)}), bf16[256,24,128]{2,1,0:T(8,128)(2,1)}, u32[]{:S(2)}, u32[]{:S(2)}) %all-to-all-start) | async-done | bytes 1572896 | tf_op jit(solution)/shard_map/all_to_all | solution.py:11
  166.8 2.2 fusion.43
  169.6 1.3 reshape.216
  171.8 2.7 %constant_dynamic-update-slice_fusion.14 = (bf16[28,192,128]{2,1,0:T(8,128)(2,1)}, bf16[12,192,128]{2,1,0:T(8,128)(2,1)}, f32[12,192,128]{2,1,0:T(8,128)}) fusion(bf16[6,12,192]{2,1,0:T(8,128)(2,1)} %reshape_squeeze.9, bf16[12,6,128]{2,0,1:T(8,128)(2,1)S(1)} %fusion.35), kind=kOutput, calls=%fused_computation.82 | convolution fusion | flops 3833855 | bytes 2405376 | tf_op jit(solution)/shard_map/knd,nkr->ndr/dot_general | solution.py:100
  174.4 2.4 %gather_fusion.13 = bf16[4,192,128]{2,1,0:T(8,128)(2,1)} fusion(bf16[12,192,128]{2,1,0:T(8,128)(2,1)} %get-tuple-element.8, s32[1024]{0:T(1024)} %pad_clamp_fusion.1), kind=kCustom, calls=%fused_computation.12.clone | custom fusion | bytes 393232 | tf_op jit(solution)/shard_map/jit(_take)/gather | solution.py:56
  176.9 2.4 %gather_fusion.12 = bf16[4,192,128]{2,1,0:T(8,128)(2,1)} fusion(bf16[12,192,128]{2,1,0:T(8,128)(2,1)} %get-tuple-element.8, s32[1024]{0:T(1024)} %pad_clamp_fusion.2), kind=kCustom, calls=%fused_computation.11.clone | custom fusion | bytes 393232 | tf_op jit(solution)/shard_map/jit(_take)/gather | solution.py:56
  179.3 2.4 %gather_fusion.11 = bf16[4,192,128]{2,1,0:T(8,128)(2,1)} fusion(bf16[12,192,128]{2,1,0:T(8,128)(2,1)} %get-tuple-element.8, s32[1024]{0:T(1024)} %pad_clamp_fusion.3), kind=kCustom, calls=%fused_computation.10.clone | custom fusion | bytes 393232 | tf_op jit(solution)/shard_map/jit(_take)/gather | solution.py:53
  181.7 2.5 %gather_fusion.10 = bf16[4,192,128]{2,1,0:T(8,128)(2,1)} fusion(bf16[12,192,128]{2,1,0:T(8,128)(2,1)} %get-tuple-element.8, s32[1024]{0:T(1024)} %pad_clamp_fusion.4), kind=kCustom, calls=%fused_computation.9.clone | custom fusion | bytes 393232 | tf_op jit(solution)/shard_map/jit(_take)/gather | solution.py:53
  187.2 2.1 collective-permute-start.9
  189.3 3.4 %collective-permute-start.8 = (bf16[4,192,128]{2,1,0:T(8,128)(2,1)S(1)}, bf16[4,192,128]{2,1,0:T(8,128)(2,1)S(1)}, u32[]{:S(2)}, u32[]{:S(2)}) collective-permute-start(bf16[4,192,128]{2,1,0:T(8,128)(2,1)S(1)} %broadcast_select_fusion.12), channel_id=1, source_target_pairs={{0,8},{8,16},{16,24},{24,32},{32,40},{40,48},{48,56},{56,64},{64,7... | collective-permute-start | bytes 589832 | tf_op jit(solution)/shard_map/ppermute | solution.py:21
  194.3 11.2 %collective-permute-done.8 = bf16[4,192,128]{2,1,0:T(8,128)(2,1)S(1)} collective-permute-done((bf16[4,192,128]{2,1,0:T(8,128)(2,1)S(1)}, bf16[4,192,128]{2,1,0:T(8,128)(2,1)S(1)}, u32[]{:S(2)}, u32[]{:S(2)}) %collective-permute-start.8) | collective-permute-done | bytes 196640 | tf_op jit(solution)/shard_map/ppermute | solution.py:21
  206.9 3.6 %collective-permute-done.10 = bf16[4,192,128]{2,1,0:T(8,128)(2,1)S(1)} collective-permute-done((bf16[4,192,128]{2,1,0:T(8,128)(2,1)S(1)}, bf16[4,192,128]{2,1,0:T(8,128)(2,1)S(1)}, u32[]{:S(2)}, u32[]{:S(2)}) %collective-permute-start.10) | collective-permute-done | bytes 196640 | tf_op jit(solution)/shard_map/ppermute | solution.py:21
  212.5 5.0 %gather_fusion.14 = bf16[96,192,128]{2,1,0:T(8,128)(2,1)} fusion(bf16[28,192,128]{2,1,0:T(8,128)(2,1)} %constant_dynamic-update-slice_fusion.10, s32[1024]{0:T(1024)} %copy-done.32), kind=kCustom, calls=%fused_computation.14.clone | custom fusion | bytes 9437568 | tf_op jit(solution)/shard_map/jit(_take)/gather | solution.py:60
  217.5 2.8 %broadcast_select_fusion = bf16[96,192,128]{2,1,0:T(8,128)(2,1)S(1)} fusion(bf16[96,192,128]{2,1,0:T(8,128)(2,1)} %gather_fusion.14, pred[96]{0:T(512)(128)(4,1)} %compare_and_fusion), kind=kLoop, calls=%fused_computation.21 | loop fusion | flops 2359296 | bytes 9437280 | tf_op jit(solution)/shard_map/jit(_take)/select_n | solution.py:60
  220.4 5.1 %fusion.21 = f32[1,1,12,192,128]{4,3,2,1,0:T(8,128)S(1)} fusion(f32[1,1,12,192,128]{4,3,2,1,0:T(8,128)S(1)} %fusion.18, bf16[12,1536,128]{2,1,0:T(8,128)(2,1)S(1)} %bitcast.102, bf16[1,1,12,192,1536]{4,3,2,1,0:T(8,128)(2,1)} %param.14), kind=kOutput, calls=%fused_computation.30 | convolution fusion | flops 906264576 | bytes 14155776 | tf_op jit(solution)/shard_map/nde,ner->ndr/dot_general | solution.py:61
  225.5 1.2 multiply_add_fusion.2
  (127 shorter events, 37.3 us)
Async XLA Ops:
  0.0 166.8 %copy-start = (bf16[192,6144]{1,0:T(8,128)(2,1)S(1)}, bf16[192,6144]{1,0:T(8,128)(2,1)}, u32[]{:S(2)}) copy-start(bf16[192,6144]{1,0:T(8,128)(2,1)} %param.19) | copy-start | bytes 7077892
  2.9 3.9 %copy-start.11 = (f32[12,64]{1,0:T(8,128)}, f32[12,64]{1,0:T(8,128)S(1)}, u32[]{:S(2)}) copy-start(f32[12,64]{1,0:T(8,128)S(1)} %get-tuple-element.30) | copy-start | bytes 9220
  2.9 3.9 %copy-start.14 = (f32[12,64]{1,0:T(8,128)}, f32[12,64]{1,0:T(8,128)S(1)}, u32[]{:S(2)}) copy-start(f32[12,64]{1,0:T(8,128)S(1)} %get-tuple-element.31) | copy-start | bytes 9220
  2.9 3.9 %copy-start.17 = (f32[12,64]{1,0:T(8,128)}, f32[12,64]{1,0:T(8,128)S(1)}, u32[]{:S(2)}) copy-start(f32[12,64]{1,0:T(8,128)S(1)} %get-tuple-element.32) | copy-start | bytes 9220
  2.9 3.9 %copy-start.20 = (f32[12,64]{1,0:T(8,128)}, f32[12,64]{1,0:T(8,128)S(1)}, u32[]{:S(2)}) copy-start(f32[12,64]{1,0:T(8,128)S(1)} %get-tuple-element.33) | copy-start | bytes 9220
  2.9 3.9 %copy-start.23 = (f32[12,64]{1,0:T(8,128)}, f32[12,64]{1,0:T(8,128)S(1)}, u32[]{:S(2)}) copy-start(f32[12,64]{1,0:T(8,128)S(1)} %get-tuple-element.34) | copy-start | bytes 9220
  3.0 3.9 %copy-start.26 = (f32[12,64]{1,0:T(8,128)}, f32[12,64]{1,0:T(8,128)S(1)}, u32[]{:S(2)}) copy-start(f32[12,64]{1,0:T(8,128)S(1)} %get-tuple-element.35) | copy-start | bytes 9220
  3.0 3.9 %copy-start.29 = (f32[12,64]{1,0:T(8,128)}, f32[12,64]{1,0:T(8,128)S(1)}, u32[]{:S(2)}) copy-start(f32[12,64]{1,0:T(8,128)S(1)} %get-tuple-element.36) | copy-start | bytes 9220
  5.9 1.0 copy-start.8
  9.0 31.6 %collective-permute-start = (bf16[4,192,128]{2,1,0:T(8,128)(2,1)}, bf16[4,192,128]{2,1,0:T(8,128)(2,1)}, u32[]{:S(2)}, u32[]{:S(2)}) collective-permute-start(bf16[4,192,128]{2,1,0:T(8,128)(2,1)} %broadcast_select_fusion.14), channel_id=1, source_target_pairs={{0,8},{8,16},{16,24},{24,32},{32,40},{40,48},{48,56},{56,64},{64,7... | collective-permute-start | bytes 589832 | tf_op jit(solution)/shard_map/ppermute | solution.py:21
  20.1 22.2 %collective-permute-start.1 = (bf16[4,192,128]{2,1,0:T(8,128)(2,1)}, bf16[4,192,128]{2,1,0:T(8,128)(2,1)}, u32[]{:S(2)}, u32[]{:S(2)}) collective-permute-start(bf16[4,192,128]{2,1,0:T(8,128)(2,1)} %broadcast_select_fusion.11), channel_id=1, source_target_pairs={{0,248},{8,0},{16,8},{24,16},{32,24},{40,32},{48,40},{56,48},{64,5... | collective-permute-start | bytes 589832 | tf_op jit(solution)/shard_map/ppermute | solution.py:21
  28.0 15.9 %collective-permute-start.2 = (bf16[4,192,128]{2,1,0:T(8,128)(2,1)}, bf16[4,192,128]{2,1,0:T(8,128)(2,1)}, u32[]{:S(2)}, u32[]{:S(2)}) collective-permute-start(bf16[4,192,128]{2,1,0:T(8,128)(2,1)} %broadcast_select_fusion.8), channel_id=1, source_target_pairs={{0,1},{1,2},{2,3},{3,4},{4,5},{5,6},{6,7},{7,0},{8,9},{9,10},{10,1... | collective-permute-start | bytes 589832 | tf_op jit(solution)/shard_map/ppermute | solution.py:21
  32.8 12.6 %collective-permute-start.3 = (bf16[4,192,128]{2,1,0:T(8,128)(2,1)}, bf16[4,192,128]{2,1,0:T(8,128)(2,1)S(1)}, u32[]{:S(2)}, u32[]{:S(2)}) collective-permute-start(bf16[4,192,128]{2,1,0:T(8,128)(2,1)} %broadcast_select_fusion.5), channel_id=1, source_target_pairs={{0,7},{1,0},{2,1},{3,2},{4,3},{5,4},{6,5},{7,6},{8,15},{9,8},{10,9... | collective-permute-start | bytes 589832 | tf_op jit(solution)/shard_map/ppermute | solution.py:21
  40.6 10.4 %copy-start.32 = (s32[1024]{0:T(1024)}, s32[1024]{0:T(1024)S(1)}, u32[]{:S(2)}) copy-start(s32[1024]{0:T(1024)S(1)} %pad_clamp_fusion) | copy-start | bytes 12292
  46.2 4.8 %copy-start.33 = (pred[96]{0:T(512)(128)(4,1)S(1)}, pred[96]{0:T(512)(128)(4,1)}, u32[]{:S(2)}) copy-start(pred[96]{0:T(512)(128)(4,1)} %compare_and_fusion) | copy-start | bytes 292
  51.0 2.9 %copy-start.3 = (f32[1,1,12,192,128]{4,3,2,1,0:T(8,128)S(1)}, f32[1,1,12,192,128]{4,3,2,1,0:T(8,128)}, u32[]{:S(2)}) copy-start(f32[1,1,12,192,128]{4,3,2,1,0:T(8,128)} %param.12) | copy-start | bytes 3538948
  54.0 5.2 %copy-start.12 = (f32[12,64]{1,0:T(8,128)S(1)}, f32[12,64]{1,0:T(8,128)}, u32[]{:S(2)}) copy-start(f32[12,64]{1,0:T(8,128)} %copy-done.11) | copy-start | bytes 9220
  54.0 5.2 %copy-start.15 = (f32[12,64]{1,0:T(8,128)S(1)}, f32[12,64]{1,0:T(8,128)}, u32[]{:S(2)}) copy-start(f32[12,64]{1,0:T(8,128)} %copy-done.14) | copy-start | bytes 9220
  54.0 5.2 %copy-start.18 = (f32[12,64]{1,0:T(8,128)S(1)}, f32[12,64]{1,0:T(8,128)}, u32[]{:S(2)}) copy-start(f32[12,64]{1,0:T(8,128)} %copy-done.17) | copy-start | bytes 9220
  54.0 5.2 %copy-start.21 = (f32[12,64]{1,0:T(8,128)S(1)}, f32[12,64]{1,0:T(8,128)}, u32[]{:S(2)}) copy-start(f32[12,64]{1,0:T(8,128)} %copy-done.20) | copy-start | bytes 9220
  54.0 5.2 %copy-start.24 = (f32[12,64]{1,0:T(8,128)S(1)}, f32[12,64]{1,0:T(8,128)}, u32[]{:S(2)}) copy-start(f32[12,64]{1,0:T(8,128)} %copy-done.23) | copy-start | bytes 9220
  54.0 5.2 %copy-start.27 = (f32[12,64]{1,0:T(8,128)S(1)}, f32[12,64]{1,0:T(8,128)}, u32[]{:S(2)}) copy-start(f32[12,64]{1,0:T(8,128)} %copy-done.26) | copy-start | bytes 9220
  54.0 5.2 %copy-start.30 = (f32[12,64]{1,0:T(8,128)S(1)}, f32[12,64]{1,0:T(8,128)}, u32[]{:S(2)}) copy-start(f32[12,64]{1,0:T(8,128)} %copy-done.29) | copy-start | bytes 9220
  59.1 2.9 %copy-start.1 = (f32[1,1,12,192,128]{4,3,2,1,0:T(8,128)}, f32[1,1,12,192,128]{4,3,2,1,0:T(8,128)S(1)}, u32[]{:S(2)}) copy-start(f32[1,1,12,192,128]{4,3,2,1,0:T(8,128)S(1)} %fusion.15) | copy-start | bytes 3538948
  59.1 1.3 copy-start.7
  59.1 1.5 copy-start.9
  67.9 14.9 %collective-permute-start.4 = (bf16[4,192,128]{2,1,0:T(8,128)(2,1)S(1)}, bf16[4,192,128]{2,1,0:T(8,128)(2,1)S(1)}, u32[]{:S(2)}, u32[]{:S(2)}) collective-permute-start(bf16[4,192,128]{2,1,0:T(8,128)(2,1)S(1)} %broadcast_select_fusion.13), channel_id=1, source_target_pairs={{0,8},{8,16},{16,24},{24,32},{32,40},{40,48},{48,56},{56,64},{64,7... | collective-permute-start | bytes 589832 | tf_op jit(solution)/shard_map/ppermute | solution.py:21
  69.7 14.2 %collective-permute-start.5 = (bf16[4,192,128]{2,1,0:T(8,128)(2,1)S(1)}, bf16[4,192,128]{2,1,0:T(8,128)(2,1)S(1)}, u32[]{:S(2)}, u32[]{:S(2)}) collective-permute-start(bf16[4,192,128]{2,1,0:T(8,128)(2,1)S(1)} %broadcast_select_fusion.10), channel_id=1, source_target_pairs={{0,248},{8,0},{16,8},{24,16},{32,24},{40,32},{48,40},{56,48},{64,5... | collective-permute-start | bytes 589832 | tf_op jit(solution)/shard_map/ppermute | solution.py:21
  78.4 11.4 %collective-permute-start.6 = (bf16[4,192,128]{2,1,0:T(8,128)(2,1)S(1)}, bf16[4,192,128]{2,1,0:T(8,128)(2,1)S(1)}, u32[]{:S(2)}, u32[]{:S(2)}) collective-permute-start(bf16[4,192,128]{2,1,0:T(8,128)(2,1)S(1)} %broadcast_select_fusion.7), channel_id=1, source_target_pairs={{0,1},{1,2},{2,3},{3,4},{4,5},{5,6},{6,7},{7,0},{8,9},{9,10},{10,1... | collective-permute-start | bytes 589832 | tf_op jit(solution)/shard_map/ppermute | solution.py:21
  80.7 13.0 %collective-permute-start.7 = (bf16[4,192,128]{2,1,0:T(8,128)(2,1)S(1)}, bf16[4,192,128]{2,1,0:T(8,128)(2,1)S(1)}, u32[]{:S(2)}, u32[]{:S(2)}) collective-permute-start(bf16[4,192,128]{2,1,0:T(8,128)(2,1)S(1)} %broadcast_select_fusion.4), channel_id=1, source_target_pairs={{0,7},{1,0},{2,1},{3,2},{4,3},{5,4},{6,5},{7,6},{8,15},{9,8},{10,9... | collective-permute-start | bytes 589832 | tf_op jit(solution)/shard_map/ppermute | solution.py:21
  94.4 5.0 %copy-start.34 = (pred[96]{0:T(512)(128)(4,1)S(1)}, pred[96]{0:T(512)(128)(4,1)}, u32[]{:S(2)}) copy-start(pred[96]{0:T(512)(128)(4,1)} %compare_and_fusion) | copy-start | bytes 292
  99.4 2.9 %copy-start.2 = (f32[1,1,12,192,128]{4,3,2,1,0:T(8,128)S(1)}, f32[1,1,12,192,128]{4,3,2,1,0:T(8,128)}, u32[]{:S(2)}) copy-start(f32[1,1,12,192,128]{4,3,2,1,0:T(8,128)} %copy-done.1) | copy-start | bytes 3538948
  102.3 5.0 %copy-start.10 = (bf16[6,12,192]{2,1,0:T(8,128)(2,1)S(1)}, bf16[6,12,192]{2,1,0:T(8,128)(2,1)}, u32[]{:S(2)}) copy-start(bf16[6,12,192]{2,1,0:T(8,128)(2,1)} %reshape_squeeze.9) | copy-start | bytes 82948
  102.3 5.3 %copy-start.35 = (s32[1,1,12]{2,1,0:T(1,128)S(1)}, s32[1,1,12]{2,1,0:T(1,128)}, u32[]{:S(2)}) copy-start(s32[1,1,12]{2,1,0:T(1,128)} %param.17) | copy-start | bytes 148
  111.8 55.0 %all-to-all-start = ((bf16[256,24,128]{2,1,0:T(8,128)(2,1)}), bf16[256,24,128]{2,1,0:T(8,128)(2,1)}, u32[]{:S(2)}, u32[]{:S(2)}) async-start(bf16[256,24,128]{2,1,0:T(8,128)(2,1)} %stack.10), calls=%async_computation | async-start | bytes 3145728 | tf_op jit(solution)/shard_map/all_to_all | solution.py:11
  187.2 19.0 %collective-permute-start.9 = (bf16[4,192,128]{2,1,0:T(8,128)(2,1)S(1)}, bf16[4,192,128]{2,1,0:T(8,128)(2,1)S(1)}, u32[]{:S(2)}, u32[]{:S(2)}) collective-permute-start(bf16[4,192,128]{2,1,0:T(8,128)(2,1)S(1)} %broadcast_select_fusion.9), channel_id=1, source_target_pairs={{0,248},{8,0},{16,8},{24,16},{32,24},{40,32},{48,40},{56,48},{64,5... | collective-permute-start | bytes 589832 | tf_op jit(solution)/shard_map/ppermute | solution.py:21
  189.3 16.2 %collective-permute-start.8 = (bf16[4,192,128]{2,1,0:T(8,128)(2,1)S(1)}, bf16[4,192,128]{2,1,0:T(8,128)(2,1)S(1)}, u32[]{:S(2)}, u32[]{:S(2)}) collective-permute-start(bf16[4,192,128]{2,1,0:T(8,128)(2,1)S(1)} %broadcast_select_fusion.12), channel_id=1, source_target_pairs={{0,8},{8,16},{16,24},{24,32},{32,40},{40,48},{48,56},{56,64},{64,7... | collective-permute-start | bytes 589832 | tf_op jit(solution)/shard_map/ppermute | solution.py:21
  193.7 16.8 %collective-permute-start.10 = (bf16[4,192,128]{2,1,0:T(8,128)(2,1)S(1)}, bf16[4,192,128]{2,1,0:T(8,128)(2,1)S(1)}, u32[]{:S(2)}, u32[]{:S(2)}) collective-permute-start(bf16[4,192,128]{2,1,0:T(8,128)(2,1)S(1)} %broadcast_select_fusion.6), channel_id=1, source_target_pairs={{0,1},{1,2},{2,3},{3,4},{4,5},{5,6},{6,7},{7,0},{8,9},{9,10},{10,1... | collective-permute-start | bytes 589832 | tf_op jit(solution)/shard_map/ppermute | solution.py:21
  193.8 18.0 %collective-permute-start.11 = (bf16[4,192,128]{2,1,0:T(8,128)(2,1)S(1)}, bf16[4,192,128]{2,1,0:T(8,128)(2,1)S(1)}, u32[]{:S(2)}, u32[]{:S(2)}) collective-permute-start(bf16[4,192,128]{2,1,0:T(8,128)(2,1)S(1)} %broadcast_select_fusion.3), channel_id=1, source_target_pairs={{0,7},{1,0},{2,1},{3,2},{4,3},{5,4},{6,5},{7,6},{8,15},{9,8},{10,9... | collective-permute-start | bytes 589832 | tf_op jit(solution)/shard_map/ppermute | solution.py:21
  220.3 5.1 %copy-start.13 = (f32[12,64]{1,0:T(8,128)S(1)}, f32[12,64]{1,0:T(8,128)}, u32[]{:S(2)}) copy-start(f32[12,64]{1,0:T(8,128)} %copy-done.11) | copy-start | bytes 9220
  220.3 5.1 %copy-start.16 = (f32[12,64]{1,0:T(8,128)S(1)}, f32[12,64]{1,0:T(8,128)}, u32[]{:S(2)}) copy-start(f32[12,64]{1,0:T(8,128)} %copy-done.14) | copy-start | bytes 9220
  220.3 5.1 %copy-start.19 = (f32[12,64]{1,0:T(8,128)S(1)}, f32[12,64]{1,0:T(8,128)}, u32[]{:S(2)}) copy-start(f32[12,64]{1,0:T(8,128)} %copy-done.17) | copy-start | bytes 9220
  220.3 5.1 %copy-start.22 = (f32[12,64]{1,0:T(8,128)S(1)}, f32[12,64]{1,0:T(8,128)}, u32[]{:S(2)}) copy-start(f32[12,64]{1,0:T(8,128)} %copy-done.20) | copy-start | bytes 9220
  220.4 5.1 %copy-start.25 = (f32[12,64]{1,0:T(8,128)S(1)}, f32[12,64]{1,0:T(8,128)}, u32[]{:S(2)}) copy-start(f32[12,64]{1,0:T(8,128)} %copy-done.23) | copy-start | bytes 9220
  220.4 5.1 %copy-start.28 = (f32[12,64]{1,0:T(8,128)S(1)}, f32[12,64]{1,0:T(8,128)}, u32[]{:S(2)}) copy-start(f32[12,64]{1,0:T(8,128)} %copy-done.26) | copy-start | bytes 9220
  220.4 5.1 %copy-start.31 = (f32[12,64]{1,0:T(8,128)S(1)}, f32[12,64]{1,0:T(8,128)}, u32[]{:S(2)}) copy-start(f32[12,64]{1,0:T(8,128)} %copy-done.29) | copy-start | bytes 9220
  226.7 1.3 copy-start.4
  226.8 1.6 copy-start.5
  (1 other events, 0.7 us)
